TPU v7x, 512 devices: a whole 4x4x16 slice. The times are simulated.
512 devices in a mesh: mpo: 8 (over y, core), sec: 64 (over x, z).
Axes of the slice: x: 4, y: 4, z: 16, core: 2. Of those that a mesh axis runs over, the one named last changes fastest.
Arguments:
- theta: bfloat16 [16, 1024, 1024], P(None, 'sec'), may hold values from -6 to 6
- env_left: bfloat16 [24, 16384, 1024], P('mpo', 'sec'), may hold values from -0.1875 to 0.1875
- env_right: bfloat16 [24, 16384, 1024], P('mpo', 'sec'), may hold values from -0.0390625 to 0.0390625
- mpo_core: float32 [24, 24], replicated, may hold values from -1.25 to 1.25
- sector_sizes: int32 [16], replicated, may hold values from 1 to 1024, 12288 in all
Outputs:
- applied: bfloat16 [1024, 16384], P('mpo', 'sec')
Inputs may be any that keep to these rules, and one draw needn't show every extreme that they name: `sector_sizes`: one sector has exactly 1024 states in use; the sizes sum to 12288.
All inputs are finite; a program needn't handle non-finite values.
Results may differ from a plain program's by a relative error of at most 0.0058.
Values may be sent and summed in bfloat16 or wider, within the bound.
No kernel may reach another device: no remote copies, remote signals or barrier semaphores. Data moves between devices by JAX's collectives and lax.ppermute only.
A program may use at most 64 MiB of HBM per device.

v0:
```python
import jax
import jax.numpy as jnp
from jax import lax
from jax.sharding import PartitionSpec as P

G = 4


def swapped(array, axis, stride):
    return lax.ppermute(array, axis, [(i, i ^ 1 << stride) for i in range(lax.axis_size(axis))])


def on_device(theta, env_left, env_right, mpo_core, sector_sizes):
    sectors = theta.shape[0]
    rows_local = theta.shape[1]
    width = theta.shape[2]
    local_w = env_left.shape[0]
    slab = env_left.shape[1]
    sec_place = lax.axis_index("sec")
    sector = sec_place // G
    block_pos = sec_place % G
    live_size = jnp.sum(jnp.where(jnp.arange(sectors, dtype=jnp.int32) == sector, sector_sizes, 0))
    bit_count = G.bit_length() - 1
    spread = jnp.broadcast_to(theta[:, None], (sectors, G, rows_local, width))
    spread = spread.reshape(sectors * G, rows_local, width)
    sector_block = lax.all_to_all(spread, "sec", split_axis=0, concat_axis=1, tiled=True)[0]
    positions = jnp.arange(width, dtype=jnp.int32)
    keep_row = positions < live_size
    sector_block = jnp.where(
        keep_row[:, None] & keep_row[None, :], sector_block, jnp.zeros_like(sector_block)
    )
    product = jnp.einsum(
        "akm,mn->akn", env_left, sector_block, preferred_element_type=jnp.float32
    ).astype(jnp.bfloat16)
    own_start = lax.axis_index("mpo") * local_w
    core_cols = lax.dynamic_slice_in_dim(mpo_core, own_start, local_w, 1)
    mixed = jnp.einsum(
        "ab,akn->bkn",
        core_cols,
        lax.all_gather(product, "mpo", axis=0, tiled=True).astype(jnp.float32),
        precision=lax.Precision.HIGHEST,
    ).astype(jnp.bfloat16)
    for bit_index in range(bit_count):
        partner = swapped(mixed, "sec", bit_index)
        upper_half = sec_place >> bit_index & 1 == 1
        mixed = jnp.where(
            upper_half, jnp.concatenate([partner, mixed], 1), jnp.concatenate([mixed, partner], 1)
        )
    col_keep = block_pos * slab + jnp.arange(slab, dtype=jnp.int32) < live_size
    sector_term = jnp.einsum("bil,bjl->ij", mixed, env_right, preferred_element_type=jnp.float32)
    row_keep = (
        jnp.arange(lax.axis_size("mpo") * (width // lax.axis_size("mpo")), dtype=jnp.int32)
        < live_size
    )
    result = lax.psum_scatter(
        jnp.where(row_keep[:, None] & col_keep[None, :], sector_term, jnp.zeros_like(sector_term)),
        "mpo",
        scatter_dimension=0,
        tiled=True,
    )
    return result.astype(jnp.bfloat16)


def solution(mesh):
    return jax.shard_map(
        on_device,
        mesh=mesh,
        in_specs=(P(None, "sec", None), P("mpo", "sec", None), P("mpo", "sec", None), P(), P()),
        out_specs=P("mpo", "sec"),
        check_vma=False,
    )
```

profile of v0, /device:TPU:2, one launch (start us, length us, event | category | flops | bytes accessed | tf_op | source)
XLA Modules:
  0.0 477.4 jit_solution(1534336615428155424)
XLA Ops:
  6.5 2.8 broadcast_in_dim.11
  9.3 18.8 %all-to-all-start = ((bf16[64,16,1024]{2,1,0:T(8,128)(2,1)}), bf16[64,16,1024]{2,1,0:T(8,128)(2,1)}, u32[]{:S(2)}, u32[]{:S(2)}) async-start(bf16[64,16,1024]{2,1,0:T(8,128)(2,1)} %bitcast.21), calls=%async_computation | async-start | bytes 4194304 | tf_op jit(solution)/shard_map/all_to_all | solution.py:26
  28.2 0.6 fusion.27
  28.8 0.6 iota_compare_fusion
  29.5 95.7 %all-to-all-done = bf16[64,16,1024]{2,1,0:T(8,128)(2,1)} async-done(((bf16[64,16,1024]{2,1,0:T(8,128)(2,1)}), bf16[64,16,1024]{2,1,0:T(8,128)(2,1)}, u32[]{:S(2)}, u32[]{:S(2)}) %all-to-all-start) | async-done | bytes 2097184 | tf_op jit(solution)/shard_map/all_to_all | solution.py:26
  125.2 4.9 %fusion.15 = bf16[3,256,1024]{2,1,0:T(8,128)(2,1)} fusion(bf16[3,256,1024]{2,1,0:T(8,128)(2,1)S(1)} %copy-done, bf16[1024,1024]{1,0:T(8,128)(2,1)} %bitcast.2, pred[1024]{0:T(1024)(128)(4,1)S(1)} %iota_compare_fusion), kind=kOutput, calls=%fused_computation.13 | convolution fusion | flops 1613496320 | bytes 5243904 | tf_op jit(solution)/shard_map/akm,mn->akn/dot_general | solution.py:32
  130.2 69.3 %all-gather.2.cloned.1.call-done = bf16[24,256,1024]{2,1,0:T(8,128)(2,1)} async-done(((bf16[3,256,1024]{2,1,0:T(8,128)(2,1)}), bf16[24,256,1024]{2,1,0:T(8,128)(2,1)}) %all-gather.2.cloned.1.call-update) | async-done | bytes 12582928 | tf_op jit(solution)/shard_map/all_gather | solution.py:40
  199.5 17.3 %fusion.9 = bf16[3,256,1024]{2,0,1:T(4,128)(2,1)S(1)} fusion(bf16[24,256,1024]{2,1,0:T(8,128)(2,1)} %all-gather.2.cloned.1.call-done, f32[24,24]{1,0:T(8,128)S(1)} %copy-done.5, s32[]{:T(128)S(6)} %select_n.47), kind=kOutput, calls=%fused_computation.11 | convolution fusion | flops 227278848 | bytes 14158084 | tf_op jit(solution)/shard_map/ab,akn->bkn/dot_general | solution.py:37
  216.8 1.3 copy-done.3
  218.1 1.8 copy.10
  219.8 3.6 collective-permute-start
  223.5 35.0 %collective-permute-done = bf16[3,256,1024]{2,1,0:T(8,128)(2,1)S(1)} collective-permute-done((bf16[3,256,1024]{2,1,0:T(8,128)(2,1)}, bf16[3,256,1024]{2,1,0:T(8,128)(2,1)S(1)}, u32[]{:S(2)}, u32[]{:S(2)}) %collective-permute-start) | collective-permute-done | bytes 1572896 | tf_op jit(solution)/shard_map/ppermute | solution.py:10
  258.5 1.4 copy.11
  259.9 4.7 maximum_select_fusion.1
  264.5 1.9 copy-done.1
  266.5 2.9 copy.13
  269.4 4.4 collective-permute-start.1
  273.9 0.8 add_compare_fusion
  274.7 134.6 %collective-permute-done.1 = bf16[3,512,1024]{2,1,0:T(8,128)(2,1)} collective-permute-done((bf16[3,512,1024]{2,1,0:T(8,128)(2,1)}, bf16[3,512,1024]{2,1,0:T(8,128)(2,1)}, u32[]{:S(2)}, u32[]{:S(2)}) %collective-permute-start.1) | collective-permute-done | bytes 3145760 | tf_op jit(solution)/shard_map/ppermute | solution.py:10
  409.3 4.6 copy.14
  413.9 9.3 %maximum_select_fusion = bf16[3,1024,1024]{2,0,1:T(4,128)(2,1)S(1)} fusion(bf16[3,512,1024]{2,0,1:T(4,128)(2,1)S(1)} %copy-done.2, bf16[3,512,1024]{2,0,1:T(4,128)(2,1)S(1)} %copy.14, pred[]{:T(512)S(6)} %eq.16), kind=kLoop, calls=%fused_computation.2 | loop fusion | flops 9437184 | bytes 12582913 | tf_op jit(solution)/shard_map/jit(_where)/select_n | solution.py:46
  423.3 5.2 %fusion.21 = f32[1024,256]{1,0:T(8,128)} fusion(bf16[3,256,1024]{2,1,0:T(8,128)(2,1)S(1)} %copy-done.6, bf16[3,1024,1024]{2,0,1:T(4,128)(2,1)S(1)} %maximum_select_fusion, pred[256]{0:T(512)(128)(4,1)S(1)} %add_compare_fusion, pred[1024]{0:T(1024)(128)(4,1)S(1)} %iota_compare_fusion), kind=kOutput, calls=%fused_computation.15 | convolution fusion | flops 1611137024 | bytes 8914176 | tf_op jit(solution)/shard_map/bil,bjl->ij/dot_general | solution.py:50
  428.5 40.5 %reduce-scatter.2.cloned.1.call-done = f32[128,256]{1,0:T(8,128)} async-done(((f32[1024,256]{1,0:T(8,128)}), f32[128,256]{1,0:T(8,128)}) %reduce-scatter.2.cloned.1.call-update) | async-done | bytes 131088 | tf_op jit(solution)/shard_map/reduce_scatter | solution.py:55
  469.0 1.5 convert_element_type.16
  (18 shorter events, 0.1 us)
Async XLA Ops:
  6.5 118.7 %copy-start = (bf16[3,256,1024]{2,1,0:T(8,128)(2,1)S(1)}, bf16[3,256,1024]{2,1,0:T(8,128)(2,1)}, u32[]{:S(2)}) copy-start(bf16[3,256,1024]{2,1,0:T(8,128)(2,1)} %param.6) | copy-start | bytes 4718596
  6.5 21.7 %copy-start.7 = (s32[16]{0:T(128)S(1)}, s32[16]{0:T(128)}, u32[]{:S(2)}) copy-start(s32[16]{0:T(128)} %param.9) | copy-start | bytes 196
  9.3 115.9 %all-to-all-start = ((bf16[64,16,1024]{2,1,0:T(8,128)(2,1)}), bf16[64,16,1024]{2,1,0:T(8,128)(2,1)}, u32[]{:S(2)}, u32[]{:S(2)}) async-start(bf16[64,16,1024]{2,1,0:T(8,128)(2,1)} %bitcast.21), calls=%async_computation | async-start | bytes 4194304 | tf_op jit(solution)/shard_map/all_to_all | solution.py:26
  28.1 171.4 %all-gather.2.cloned.1.call-start = ((), (), s32[]{:S(2)}) async-start(), calls=%async_computation.2 | async-start | bytes 14155776 | tf_op jit(solution)/shard_map/all_gather | solution.py:40
  125.2 74.3 %copy-start.5 = (f32[24,24]{1,0:T(8,128)S(1)}, f32[24,24]{1,0:T(8,128)}, u32[]{:S(2)}) copy-start(f32[24,24]{1,0:T(8,128)} %param.8) | copy-start | bytes 6916
  130.1 338.9 %reduce-scatter.2.cloned.1.call-start = ((), (), s32[]{:S(2)}) async-start(), calls=%async_computation.3 | async-start | bytes 1179648 | tf_op jit(solution)/shard_map/reduce_scatter | solution.py:55
  216.8 1.3 copy-start.3
  219.8 38.6 %collective-permute-start = (bf16[3,256,1024]{2,1,0:T(8,128)(2,1)}, bf16[3,256,1024]{2,1,0:T(8,128)(2,1)S(1)}, u32[]{:S(2)}, u32[]{:S(2)}) collective-permute-start(bf16[3,256,1024]{2,1,0:T(8,128)(2,1)} %copy.10), channel_id=1, source_target_pairs={{0,1},{1,0},{2,3},{3,2},{4,5},{5,4},{6,7},{7,6},{8,9},{9,8},{10,11... | collective-permute-start | bytes 4718600 | tf_op jit(solution)/shard_map/ppermute | solution.py:10
  223.5 36.4 %copy-start.4 = (bf16[3,256,1024]{2,0,1:T(4,128)(2,1)S(1)}, bf16[3,256,1024]{2,0,1:T(4,128)(2,1)}, u32[]{:S(2)}) copy-start(bf16[3,256,1024]{2,0,1:T(4,128)(2,1)} %copy-done.3) | copy-start | bytes 4718596
  264.5 2.0 copy-start.1
  269.4 139.9 %collective-permute-start.1 = (bf16[3,512,1024]{2,1,0:T(8,128)(2,1)}, bf16[3,512,1024]{2,1,0:T(8,128)(2,1)}, u32[]{:S(2)}, u32[]{:S(2)}) collective-permute-start(bf16[3,512,1024]{2,1,0:T(8,128)(2,1)} %copy.13), channel_id=1, source_target_pairs={{0,2},{1,3},{2,0},{3,1},{4,6},{5,7},{6,4},{7,5},{8,10},{9,11},{10,... | collective-permute-start | bytes 9437192 | tf_op jit(solution)/shard_map/ppermute | solution.py:10
  273.9 140.0 %copy-start.2 = (bf16[3,512,1024]{2,0,1:T(4,128)(2,1)S(1)}, bf16[3,512,1024]{2,0,1:T(4,128)(2,1)}, u32[]{:S(2)}) copy-start(bf16[3,512,1024]{2,0,1:T(4,128)(2,1)} %copy-done.1) | copy-start | bytes 9437188
  413.9 9.3 %copy-start.6 = (bf16[3,256,1024]{2,1,0:T(8,128)(2,1)S(1)}, bf16[3,256,1024]{2,1,0:T(8,128)(2,1)}, u32[]{:S(2)}) copy-start(bf16[3,256,1024]{2,1,0:T(8,128)(2,1)} %param.7) | copy-start | bytes 4718596
Sparse Core Ops, SparseCore 0:
  130.3 69.1 all-gather.1
  428.7 40.3 reduce-scatter.1
where the time goes:
time: 478 us; the launch traced here: 477 us
  waiting for transfers between devices  375 us (78%)
  matrix products  27.4 us (6%)
  starting transfers between devices  27 us (6%)
  other arithmetic  17.6 us (4%)
  local copies, waits for them, and re-layouts  16.7 us (3%)
  between operations  13.6 us (3%)
    ppermute x2, waiting for transfers between devices, swapped(): lax.ppermute(array, axis, [(i, i ^ 1 << stride) for i in range(lax.axis_s...  170 us
    all_to_all x1, waiting for transfers between devices, on_device(): lax.all_to_all(spread, 'sec', split_axis=0, concat_axis=1, tiled=True)[0]  95.7 us
    all_gather x1, waiting for transfers between devices, on_device(): lax.all_gather(product, 'mpo', axis=0, tiled=True).astype(jnp.float32)  69.3 us
    reduce_scatter x1, waiting for transfers between devices, on_device(): lax.psum_scatter(jnp.where(row_keep[:, None] & col_keep[None, :], sector_...  40.5 us
    all_to_all x1, starting transfers between devices, on_device(): lax.all_to_all(spread, 'sec', split_axis=0, concat_axis=1, tiled=True)[0]  18.8 us
    dot_general x1, matrix products, on_device(): jnp.einsum('ab,akn->bkn', core_cols, lax.all_gather(product, 'mpo', axis=...  17.3 us
    select_n x2, other arithmetic, on_device(): jnp.where(upper_half, jnp.concatenate([partner, mixed], 1), jnp.concatena...  14 us
  transfers between devices with their start and end apart: 5, of which 5 were waited for; matrix products, arithmetic and copies ran while one was open for 0% of the time, Pallas kernels for 0%

commit v1 on v0

--- a/solution.py
+++ b/solution.py
@@ -2,6 +2,7 @@
 import jax.numpy as jnp
 from jax import lax
 from jax.sharding import PartitionSpec as P
+from jax.lax import all_to_all, axis_size
 
 G = 4
 
@@ -34,10 +35,17 @@
     ).astype(jnp.bfloat16)
     own_start = lax.axis_index("mpo") * local_w
     core_cols = lax.dynamic_slice_in_dim(mpo_core, own_start, local_w, 1)
+
+    def launch_copies_here(patch, which_axis):
+        return jnp.concatenate(
+            all_to_all(jnp.stack([patch for _ in range(axis_size(which_axis))]), which_axis, 0, 0),
+            axis=0,
+        )
+
     mixed = jnp.einsum(
         "ab,akn->bkn",
         core_cols,
-        lax.all_gather(product, "mpo", axis=0, tiled=True).astype(jnp.float32),
+        launch_copies_here(product, "mpo").astype(jnp.float32),
         precision=lax.Precision.HIGHEST,
     ).astype(jnp.bfloat16)
     for bit_index in range(bit_count):

time: 478 us -> 548 us (1.15)
  waiting for transfers between devices: 375 us -> 435 us
  starting transfers between devices: 27 us -> 33.1 us
  local copies, waits for them, and re-layouts: 16.7 us -> 22.5 us
    all_to_all x0 -> x1, waiting for transfers between devices: none -> 139 us  [launch_copies_here(): all_to_all(jnp.stack([patch for _ in range(axis_size(which_axis))]), whic...]
    all_gather x1 -> x0, waiting for transfers between devices: 69.3 us -> none  [on_device(): lax.all_gather(product, 'mpo', axis=0, tiled=True).astype(jnp.float32)]
    reduce_scatter x1, waiting for transfers between devices: 40.5 us -> 31.3 us  [on_device(): lax.psum_scatter(jnp.where(row_keep[:, None] & col_keep[None, :], sector_...]
    another operation x0 -> x1, local copies, waits for them, and re-layouts: none -> 6.13 us  [launch_copies_here(): jnp.stack([patch for _ in range(axis_size(which_axis))])]
    all_to_all x0 -> x1, starting transfers between devices: none -> 5.49 us  [launch_copies_here(): all_to_all(jnp.stack([patch for _ in range(axis_size(which_axis))]), whic...]
where the time goes in v1:
time: 548 us
  waiting for transfers between devices  435 us (79%)
  starting transfers between devices  33.1 us (6%)
  matrix products  26.1 us (5%)
  local copies, waits for them, and re-layouts  22.5 us (4%)
  other arithmetic  17.6 us (3%)
  between operations  13.6 us (2%)
    ppermute x2, waiting for transfers between devices, swapped(): lax.ppermute(array, axis, [(i, i ^ 1 << stride) for i in range(lax.axis_s...  168 us
    all_to_all x1, waiting for transfers between devices, launch_copies_here(): all_to_all(jnp.stack([patch for _ in range(axis_size(which_axis))]), whic...  139 us
    all_to_all x1, waiting for transfers between devices, on_device(): lax.all_to_all(spread, 'sec', split_axis=0, concat_axis=1, tiled=True)[0]  95.8 us
    reduce_scatter x1, waiting for transfers between devices, on_device(): lax.psum_scatter(jnp.where(row_keep[:, None] & col_keep[None, :], sector_...  31.3 us
    all_to_all x1, starting transfers between devices, on_device(): lax.all_to_all(spread, 'sec', split_axis=0, concat_axis=1, tiled=True)[0]  18.8 us
    dot_general x1, matrix products, on_device(): jnp.einsum('ab,akn->bkn', core_cols, launch_copies_here(product, 'mpo').a...  17.3 us
    select_n x2, other arithmetic, on_device(): jnp.where(upper_half, jnp.concatenate([partner, mixed], 1), jnp.concatena...  14 us
  transfers between devices with their start and end apart: 5, of which 5 were waited for; matrix products, arithmetic and copies ran while one was open for 0% of the time, Pallas kernels for 0%

profile of v1, /device:TPU:2, one launch (start us, length us, event | category | flops | bytes accessed | tf_op | source)
XLA Modules:
  0.0 547.9 jit_solution(10558867444505889165)
XLA Ops:
  6.5 2.8 broadcast_in_dim.11
  9.3 18.8 %all-to-all-start = ((bf16[64,16,1024]{2,1,0:T(8,128)(2,1)}), bf16[64,16,1024]{2,1,0:T(8,128)(2,1)}, u32[]{:S(2)}, u32[]{:S(2)}) async-start(bf16[64,16,1024]{2,1,0:T(8,128)(2,1)} %bitcast.22), calls=%async_computation | async-start | bytes 4194304 | tf_op jit(solution)/shard_map/all_to_all | solution.py:27
  29.5 95.8 %all-to-all-done = bf16[64,16,1024]{2,1,0:T(8,128)(2,1)} async-done(((bf16[64,16,1024]{2,1,0:T(8,128)(2,1)}), bf16[64,16,1024]{2,1,0:T(8,128)(2,1)}, u32[]{:S(2)}, u32[]{:S(2)}) %all-to-all-start) | async-done | bytes 2097184 | tf_op jit(solution)/shard_map/all_to_all | solution.py:27
  125.2 3.6 fusion.15
  128.9 0.9 copy.17
  129.8 6.1 %stack.2 = bf16[8,3,256,1024]{3,2,1,0:T(8,128)(2,1)} broadcast(bf16[3,256,1024]{2,1,0:T(8,128)(2,1)S(1)} %copy.17), dimensions={1,2,3} | broadcast | bytes 14155776 | tf_op jit(solution)/shard_map/stack | solution.py:41
  135.9 5.5 %all-to-all-start.1 = ((bf16[8,3,256,1024]{3,2,1,0:T(8,128)(2,1)}), bf16[8,3,256,1024]{3,2,1,0:T(8,128)(2,1)}, u32[]{:S(2)}, u32[]{:S(2)}) async-start(bf16[8,3,256,1024]{3,2,1,0:T(8,128)(2,1)} %stack.2), calls=%async_computation.1 | async-start | bytes 25165824 | tf_op jit(solution)/shard_map/all_to_all | solution.py:41
  141.5 139.5 %all-to-all-done.1 = bf16[8,3,256,1024]{3,2,1,0:T(8,128)(2,1)} async-done(((bf16[8,3,256,1024]{3,2,1,0:T(8,128)(2,1)}), bf16[8,3,256,1024]{3,2,1,0:T(8,128)(2,1)}, u32[]{:S(2)}, u32[]{:S(2)}) %all-to-all-start.1) | async-done | bytes 12582944 | tf_op jit(solution)/shard_map/all_to_all | solution.py:41
  280.9 17.3 %fusion.9 = bf16[3,256,1024]{2,0,1:T(4,128)(2,1)S(1)} fusion(bf16[24,256,1024]{2,1,0:T(8,128)(2,1)} %bitcast.5, f32[24,24]{1,0:T(8,128)S(1)} %copy-done.6, s32[]{:T(128)S(6)} %select_n.47), kind=kOutput, calls=%fused_computation.11 | convolution fusion | flops 227278848 | bytes 14158084 | tf_op jit(solution)/shard_map/ab,akn->bkn/dot_general | solution.py:45
  298.2 1.3 copy-done.4
  300.1 4.5 collective-permute-start
  304.7 33.9 %collective-permute-done = bf16[3,256,1024]{2,1,0:T(8,128)(2,1)S(1)} collective-permute-done((bf16[3,256,1024]{2,1,0:T(8,128)(2,1)S(1)}, bf16[3,256,1024]{2,1,0:T(8,128)(2,1)S(1)}, u32[]{:S(2)}, u32[]{:S(2)}) %collective-permute-start) | collective-permute-done | bytes 1572896 | tf_op jit(solution)/shard_map/ppermute | solution.py:11
  338.6 1.4 copy.20
  339.9 4.7 maximum_select_fusion.1
  344.6 1.9 copy-done.2
  346.6 2.9 copy.22
  349.5 4.2 collective-permute-start.1
  353.7 0.8 add_compare_fusion
  354.5 134.4 %collective-permute-done.1 = bf16[3,512,1024]{2,1,0:T(8,128)(2,1)} collective-permute-done((bf16[3,512,1024]{2,1,0:T(8,128)(2,1)}, bf16[3,512,1024]{2,1,0:T(8,128)(2,1)}, u32[]{:S(2)}, u32[]{:S(2)}) %collective-permute-start.1) | collective-permute-done | bytes 3145760 | tf_op jit(solution)/shard_map/ppermute | solution.py:11
  489.0 4.6 copy.23
  493.6 9.3 %maximum_select_fusion = bf16[3,1024,1024]{2,0,1:T(4,128)(2,1)S(1)} fusion(bf16[3,512,1024]{2,0,1:T(4,128)(2,1)S(1)} %copy-done.3, bf16[3,512,1024]{2,0,1:T(4,128)(2,1)S(1)} %copy.23, pred[]{:T(512)S(6)} %eq.16), kind=kLoop, calls=%fused_computation.2 | loop fusion | flops 9437184 | bytes 12582913 | tf_op jit(solution)/shard_map/jit(_where)/select_n | solution.py:54
  503.0 5.2 fusion.21
  508.2 31.3 %reduce-scatter.2.cloned.1.call-done = f32[128,256]{1,0:T(8,128)} async-done(((f32[1024,256]{1,0:T(8,128)}), f32[128,256]{1,0:T(8,128)}) %reduce-scatter.2.cloned.1.call-update) | async-done | bytes 131088 | tf_op jit(solution)/shard_map/reduce_scatter | solution.py:63
  539.5 1.5 convert_element_type.16
  (21 shorter events, 2.0 us)
Async XLA Ops:
  6.5 118.7 %copy-start = (bf16[3,256,1024]{2,1,0:T(8,128)(2,1)S(1)}, bf16[3,256,1024]{2,1,0:T(8,128)(2,1)}, u32[]{:S(2)}) copy-start(bf16[3,256,1024]{2,1,0:T(8,128)(2,1)} %param.6) | copy-start | bytes 4718596
  6.5 21.6 %copy-start.8 = (s32[16]{0:T(128)S(1)}, s32[16]{0:T(128)}, u32[]{:S(2)}) copy-start(s32[16]{0:T(128)} %param.9) | copy-start | bytes 196
  9.3 115.9 %all-to-all-start = ((bf16[64,16,1024]{2,1,0:T(8,128)(2,1)}), bf16[64,16,1024]{2,1,0:T(8,128)(2,1)}, u32[]{:S(2)}, u32[]{:S(2)}) async-start(bf16[64,16,1024]{2,1,0:T(8,128)(2,1)} %bitcast.22), calls=%async_computation | async-start | bytes 4194304 | tf_op jit(solution)/shard_map/all_to_all | solution.py:27
  135.9 145.0 %copy-start.6 = (f32[24,24]{1,0:T(8,128)S(1)}, f32[24,24]{1,0:T(8,128)}, u32[]{:S(2)}) copy-start(f32[24,24]{1,0:T(8,128)} %param.8) | copy-start | bytes 6916
  135.9 145.0 %all-to-all-start.1 = ((bf16[8,3,256,1024]{3,2,1,0:T(8,128)(2,1)}), bf16[8,3,256,1024]{3,2,1,0:T(8,128)(2,1)}, u32[]{:S(2)}, u32[]{:S(2)}) async-start(bf16[8,3,256,1024]{3,2,1,0:T(8,128)(2,1)} %stack.2), calls=%async_computation.1 | async-start | bytes 25165824 | tf_op jit(solution)/shard_map/all_to_all | solution.py:41
  141.4 398.1 %reduce-scatter.2.cloned.1.call-start = ((), (), s32[]{:S(2)}) async-start(), calls=%async_computation.3 | async-start | bytes 1179648 | tf_op jit(solution)/shard_map/reduce_scatter | solution.py:63
  298.2 1.3 copy-start.4
  300.1 38.4 %collective-permute-start = (bf16[3,256,1024]{2,1,0:T(8,128)(2,1)S(1)}, bf16[3,256,1024]{2,1,0:T(8,128)(2,1)S(1)}, u32[]{:S(2)}, u32[]{:S(2)}) collective-permute-start(bf16[3,256,1024]{2,1,0:T(8,128)(2,1)S(1)} %copy.19), channel_id=1, source_target_pairs={{0,1},{1,0},{2,3},{3,2},{4,5},{5,4},{6,7},{7,6},{8,9},{9,8},{10,11... | collective-permute-start | bytes 4718600 | tf_op jit(solution)/shard_map/ppermute | solution.py:11
  304.7 35.3 %copy-start.5 = (bf16[3,256,1024]{2,0,1:T(4,128)(2,1)S(1)}, bf16[3,256,1024]{2,0,1:T(4,128)(2,1)}, u32[]{:S(2)}) copy-start(bf16[3,256,1024]{2,0,1:T(4,128)(2,1)} %copy-done.4) | copy-start | bytes 4718596
  344.6 2.0 copy-start.2
  349.5 139.5 %collective-permute-start.1 = (bf16[3,512,1024]{2,1,0:T(8,128)(2,1)}, bf16[3,512,1024]{2,1,0:T(8,128)(2,1)}, u32[]{:S(2)}, u32[]{:S(2)}) collective-permute-start(bf16[3,512,1024]{2,1,0:T(8,128)(2,1)} %copy.22), channel_id=1, source_target_pairs={{0,2},{1,3},{2,0},{3,1},{4,6},{5,7},{6,4},{7,5},{8,10},{9,11},{10,... | collective-permute-start | bytes 9437192 | tf_op jit(solution)/shard_map/ppermute | solution.py:11
  353.7 139.9 %copy-start.3 = (bf16[3,512,1024]{2,0,1:T(4,128)(2,1)S(1)}, bf16[3,512,1024]{2,0,1:T(4,128)(2,1)}, u32[]{:S(2)}) copy-start(bf16[3,512,1024]{2,0,1:T(4,128)(2,1)} %copy-done.2) | copy-start | bytes 9437188
  493.6 9.3 %copy-start.7 = (bf16[3,256,1024]{2,1,0:T(8,128)(2,1)S(1)}, bf16[3,256,1024]{2,1,0:T(8,128)(2,1)}, u32[]{:S(2)}) copy-start(bf16[3,256,1024]{2,1,0:T(8,128)(2,1)} %param.7) | copy-start | bytes 4718596
  502.9 38.1 %copy-start.1 = (bf16[3,256,1024]{2,1,0:T(8,128)(2,1)S(1)}, bf16[3,256,1024]{2,1,0:T(8,128)(2,1)}, u32[]{:S(2)}) copy-start(bf16[3,256,1024]{2,1,0:T(8,128)(2,1)} %param.6) | copy-start | bytes 4718596
Sparse Core Ops, SparseCore 0:
  508.3 31.1 reduce-scatter.1
